TPU v7x, 256 devices: a whole 4x4x8 slice. The times are simulated.
256 devices in a mesh: seq: 64 (over z_hi, y, x, core), tp: 4 (over z_lo).
Axes of the slice: x: 4, y: 4, z: 8 (z_hi: 2, z_lo: 4; z = z_hi * 4 + z_lo), core: 2. Of those that a mesh axis runs over, the one named last changes fastest.
Arguments:
- residual: bfloat16 [32768, 2048], P('seq', 'tp'), may hold values from -6 to 6
- norm_gain: float32 [2048], replicated, may hold values from 0.3 to 3
- query_weight: bfloat16 [2048, 1024], P(None, 'tp'), as said below
- key_weight: bfloat16 [2048, 1024], P(None, 'tp'), as said below
- value_weight: bfloat16 [2048, 1024], P(None, 'tp'), may hold values from -0.375 to 0.375
- out_weight: bfloat16 [1024, 2048], P('tp'), may hold values from -0.1875 to 0.1875
- segment_start: int32 [32768], P('seq'), may hold values from 0 to 32640, as said below
- token_valid: int32 [32768], P('seq'), may hold values from 0 to 1, as said below
- page_slot: int32 [256], P('seq'), may hold values from 4 to 511, as said below
Outputs:
- hidden: bfloat16 [32768, 2048], P('seq', 'tp')
- cache: bfloat16 [512, 128, 2048], P('seq', None, 'tp')
Inputs may be any that keep to these rules, and one draw needn't show every extreme that they name: `segment_start`: prompts start at multiples of 128 and are contiguous; each holds at most 8192 tokens and one holds exactly 8192. `token_valid`: zeros form a tail of the last page of a prompt; the first token of every prompt is 1. No two pages share a cache page; page_slot // 8 is the device that holds the page's tokens, or the next device when that one holds tokens of the same prompt. `query_weight`: independent entries whose scale falls as the inverse square root of 2048. `key_weight`: independent entries whose scale falls as the inverse square root of 2048.
All inputs are finite; a program needn't handle non-finite values.
Results may differ from a plain program's by a relative error of at most 0.02.
The roundings to bfloat16 on the way count: a program that leaves them out, or rounds other values in their place, can miss the bound.
Values may be sent and summed in bfloat16 or wider, within the bound.
No kernel may reach another device: no remote copies, remote signals or barrier semaphores. Data moves between devices by JAX's collectives and lax.ppermute only.
A program may use at most 128 MiB of HBM per device.

v0:
```python
import jax
import jax.numpy as jnp
from jax import lax
from jax.experimental import pallas as pl
from jax.experimental.pallas import tpu as pltpu
from jax.sharding import PartitionSpec as P

HD = 64
PAGE = 128
SPAN = 16


THETA = 130000.0
EPS = 1e-05
SCALE = HD ** (-0.5)


def _step_kernel(kstart_ref, kbias_ref, seg_ref, tpos_ref, q_ref, kv_ref, s_ref, out_ref):
    q = q_ref[...]
    kv = kv_ref[...]
    rows, width = out_ref.shape
    keys = kv.shape[0]
    scores = lax.dot_general(
        q, kv[:, :HD], (((1,), (1,)), ((), ())), preferred_element_type=jnp.float32
    ) * SCALE
    krow = kstart_ref[0] + lax.broadcasted_iota(jnp.int32, (1, keys), 1) + kbias_ref[...]
    allowed = (krow >= seg_ref[...]) & (krow <= tpos_ref[...])
    state = s_ref[...]
    m_old = state[:, 0:1]
    l_old = state[:, 1:2]
    block_max = jnp.max(jnp.where(allowed, scores, -1e30), axis=1, keepdims=True)
    m_new = jnp.maximum(m_old, block_max)
    weights = jnp.where(allowed, jnp.exp(scores - m_new), 0.0)
    shrink = jnp.exp(m_old - m_new)
    l_new = l_old * shrink + jnp.sum(weights, axis=1, keepdims=True)
    update = jnp.dot(weights.astype(jnp.bfloat16), kv, preferred_element_type=jnp.float32)
    lane = lax.broadcasted_iota(jnp.int32, (rows, width), 1)
    acc = state * shrink + update
    out_ref[...] = jnp.where(lane >= HD, acc, jnp.where(lane == 0, m_new, jnp.where(lane == 1, l_new, 0.0)))


def attend_step(kstart, kbias, seg_col, tpos_col, q_hm, kv_hm, state):
    heads, rows, _ = q_hm.shape
    keys = kv_hm.shape[1]
    width = kv_hm.shape[2]
    grid_spec = pltpu.PrefetchScalarGridSpec(
        num_scalar_prefetch=1,
        grid=(heads,),
        in_specs=[
            pl.BlockSpec((1, keys), lambda h, ks: (0, 0)),
            pl.BlockSpec((rows, 1), lambda h, ks: (0, 0)),
            pl.BlockSpec((rows, 1), lambda h, ks: (0, 0)),
            pl.BlockSpec((None, rows, HD), lambda h, ks: (h, 0, 0)),
            pl.BlockSpec((None, keys, width), lambda h, ks: (h, 0, 0)),
            pl.BlockSpec((None, rows, width), lambda h, ks: (h, 0, 0)),
        ],
        out_specs=pl.BlockSpec((None, rows, width), lambda h, ks: (h, 0, 0)),
    )
    flops = heads * rows * keys * (2 * HD + 2 * width)
    return pl.pallas_call(
        _step_kernel,
        grid_spec=grid_spec,
        out_shape=jax.ShapeDtypeStruct(state.shape, jnp.float32),
        input_output_aliases={6: 0},
        cost_estimate=pl.CostEstimate(
            flops=flops,
            transcendentals=heads * rows * keys,
            bytes_accessed=q_hm.size * 2 + kv_hm.size * 2 + state.size * 8,
        ),
    )(kstart, kbias, seg_col, tpos_col, q_hm, kv_hm, state)


def passed_along(x, axis, by):
    count = lax.axis_size(axis)
    pairs = [(i, i + by) for i in range(count) if 0 <= i + by < count]
    return lax.ppermute(x, axis, pairs)


def rotate(inputs, positions):
    half_dim = inputs.shape[-1] // 2
    frequency = THETA ** (-2.0 * jnp.arange(half_dim, dtype=jnp.float32) / inputs.shape[-1])
    angles = positions.astype(jnp.float32)[:, None] * frequency[None, :]
    cosine = jnp.cos(angles)[:, None, :]
    sine_part = jnp.sin(angles)[:, None, :]
    front_half = inputs[..., :half_dim]
    back_half = inputs[..., half_dim:]
    return jnp.concatenate(
        [front_half * cosine - back_half * sine_part, back_half * cosine + front_half * sine_part],
        axis=-1,
    )


def body(
    residual,
    norm_gain,
    query_weight,
    key_weight,
    value_weight,
    out_weight,
    segment_start,
    token_valid,
    page_slot,
):
    row_count = residual.shape[0]
    local_heads = query_weight.shape[1] // HD
    gathered = lax.all_gather(residual, "tp", axis=1, tiled=True)
    widened = gathered.astype(jnp.float32)
    mean_sq = jnp.mean(widened * widened, axis=1, keepdims=True)
    normed = (widened * lax.rsqrt(mean_sq + EPS) * norm_gain[None, :]).astype(jnp.bfloat16)
    seq_rank = lax.axis_index("seq")
    first_row = seq_rank * row_count
    places = first_row + jnp.arange(row_count, dtype=jnp.int32)
    offsets = places - segment_start
    queries = jnp.dot(normed, query_weight, preferred_element_type=jnp.float32).reshape(
        row_count, local_heads, HD
    )
    queries = rotate(queries, offsets).astype(jnp.bfloat16)
    key_rot = jnp.dot(normed, key_weight, preferred_element_type=jnp.float32).reshape(
        row_count, local_heads, HD
    )
    key_rot = rotate(key_rot, offsets).astype(jnp.bfloat16)
    values = (
        jnp.dot(normed, value_weight, preferred_element_type=jnp.float32)
        .reshape(row_count, local_heads, HD)
        .astype(jnp.bfloat16)
    )
    packed = jnp.concatenate([key_rot[:, :, None, :], values[:, :, None, :]], axis=2).reshape(
        row_count, local_heads * 2 * HD
    )
    packed = jnp.where(token_valid[:, None] > 0, packed, jnp.zeros_like(packed))

    out_cols = lax.all_to_all(out_weight, "tp", 1, 0, tiled=True)
    prev_slot = passed_along(page_slot, "seq", 1)

    q_hm = jnp.transpose(queries, (1, 0, 2))
    kv_hm = jnp.transpose(packed.reshape(row_count, local_heads, 2 * HD), (1, 0, 2))
    seg_col = segment_start[:, None]
    tpos_col = places[:, None]
    own_bias = jnp.where(token_valid > 0, 0, 1 << 30).astype(jnp.int32)[None, :]
    remote_bias = jnp.zeros((1, row_count), jnp.int32)

    def absorb(state, incoming, step, bias):
        kstart = (first_row - step * row_count).astype(jnp.int32).reshape(1)
        return attend_step(kstart, bias, seg_col, tpos_col, q_hm, incoming, state)

    lane = jnp.arange(2 * HD, dtype=jnp.int32)
    initial = jnp.broadcast_to(
        jnp.where(lane == 0, -1e30, 0.0).astype(jnp.float32), (local_heads, row_count, 2 * HD)
    )
    seq_count = lax.axis_size("seq")
    reach_dev = min(SPAN, seq_count // 2)
    half = seq_count // 2
    chain = [(i, i + 1) for i in range(seq_count - 1)]
    inner = [p for p in chain if p != (half - 1, half)]
    first_block = segment_start[0] // row_count
    cross_here = jnp.clip(seq_rank - first_block, 0, reach_dev).astype(jnp.int32)
    cross_steps = lax.psum(jnp.where(seq_rank == half, cross_here, 0), "seq")
    cross_steps = jnp.maximum(cross_steps, 1)

    prev_block = lax.ppermute(kv_hm, "seq", chain)
    carried = absorb(initial, kv_hm, 0, own_bias)

    def step_with(pairs):
        def advance(step_index, carry_in):
            held, state = carry_in
            sent = lax.ppermute(held, "seq", pairs)
            state = absorb(state, held, step_index, remote_bias)
            return (sent, state)

        return advance

    held, carried = lax.fori_loop(1, cross_steps, step_with(chain), (prev_block, carried))
    held, carried = lax.fori_loop(cross_steps, reach_dev, step_with(inner), (held, carried))
    carried = absorb(carried, held, reach_dev, remote_bias)
    attended = (
        jnp.transpose(carried[:, :, HD:] / carried[:, :, 1:2], (1, 0, 2))
        .astype(jnp.bfloat16)
        .reshape(row_count, local_heads * HD)
    )

    tiles = page_slot.shape[0]
    slot_count = 2 * tiles
    base_slot = seq_rank * slot_count
    has_prev = seq_rank > 0
    cand_slot = jnp.concatenate([page_slot, jnp.where(has_prev, prev_slot, -1)]) - base_slot
    cand_pages = jnp.concatenate(
        [packed.reshape(tiles, PAGE, -1), jnp.transpose(prev_block, (1, 0, 2)).reshape(tiles, PAGE, -1)],
        axis=0,
    )
    match = cand_slot[None, :] == jnp.arange(slot_count, dtype=jnp.int32)[:, None]
    pick = jnp.argmax(match.astype(jnp.int32), axis=1)
    found = jnp.any(match, axis=1)
    cache_pages = jnp.where(found[:, None, None], cand_pages[pick], jnp.zeros_like(cand_pages[:1]))

    attended_all = lax.all_gather(attended, "tp", axis=1, tiled=True)
    projected = jnp.dot(attended_all, out_cols, preferred_element_type=jnp.float32)
    hidden = (residual.astype(jnp.float32) + projected).astype(jnp.bfloat16)
    return (hidden, cache_pages)


def solution(mesh):
    return jax.shard_map(
        body,
        mesh=mesh,
        in_specs=(
            P("seq", "tp"),
            P(),
            P(None, "tp"),
            P(None, "tp"),
            P(None, "tp"),
            P("tp", None),
            P("seq"),
            P("seq"),
            P("seq"),
        ),
        out_specs=(P("seq", "tp"), P("seq", None, "tp")),
        check_vma=False,
    )
```

profile of v0, /device:TPU:24, one launch (start us, length us, event | category | flops | bytes accessed | tf_op | source)
XLA Modules:
  0.0 388.4 jit_solution(174366732571517311)
XLA Ops:
  11.7 50.8 %all-gather.3.cloned.1.call-done = bf16[512,2048]{1,0:T(8,128)(2,1)} async-done(((bf16[512,512]{1,0:T(8,128)(2,1)}), bf16[512,2048]{1,0:T(8,128)(2,1)}) %all-gather.3.cloned.1.call-update) | async-done | bytes 2097168 | tf_op jit(solution)/shard_map/all_gather | solution.py:106
  62.5 2.2 fusion.4
  66.4 2.8 fusion.14
  70.0 2.3 copy.68
  73.6 3.5 convolution_convert_fusion
  77.1 2.0 copy.51
  79.1 3.2 fusion.9
  85.2 1.9 collective-permute-start.2
  87.1 3.5 collective-permute-start.3
  93.7 2.3 copy.59
  96.0 4.2 %all-to-all-start = ((bf16[256,4,512]{0,2,1:T(8,128)(2,1)}), bf16[256,4,512]{0,2,1:T(8,128)(2,1)}, u32[]{:S(2)}, u32[]{:S(2)}) async-start(bf16[256,4,512]{0,2,1:T(8,128)(2,1)} %bitcast.15), calls=%async_computation | async-start | bytes 2097152 | tf_op jit(solution)/shard_map/all_to_all | solution.py:132
  100.3 22.7 %psum.7 = s32[]{:T(128)} all-reduce(s32[]{:T(128)S(6)} %select_n.45), channel_id=1, replica_groups=mesh['seq'=64,'tp'=4] {'seq'}, use_global_device_ids=true, to_apply=%region_1.2 | all-reduce | flops 1 | bytes 8 | tf_op jit(solution)/shard_map/psum | solution.py:157
  126.1 6.2 %shard_map.104 = f32[4,512,128]{2,1,0:T(8,128)S(1)} custom-call(s32[1]{0:T(128)} %bitcast.11.kstart_ref, s32[1,512]{1,0:T(1,128)} %bitcast.42, s32[512,1]{1,0:T(8,128)S(1)} %copy.57.seg_ref, s32[512,1]{1,0:T(8,128)} %iota_add_fusion.2.tpos_ref, bf16[4,512,64]{2,1,0:T(8,128)(2,1)S(1)} %maximum_bitcast_fusion.q_ref, ...), custom_call_target="tpu_custom_call", output_to_operand_aliasing={{}: (6, {})} | custom-call | flops 402653184 | bytes 2883584 | tf_op jit(solution)/shard_map/pallas_call | solution.py:60
  133.4 204.0 %while.29 = (s32[]{:T(128)}, bf16[4,512,128]{2,1,0:T(8,128)(2,1)S(1)}, f32[4,512,128]{2,1,0:T(8,128)S(1)}, s32[]{:T(128)}, s32[512,1]{1,0:T(8,128)S(1)}, /*index...) while((s32[]{:T(128)}, bf16[4,512,128]{2,1,0:T(8,128)(2,1)S(1)}, ...), condition=%wide.region_5.6_spmd.clone.clone, body=%wide.region_4.5_spmd.clone.clone.sunk | while | flops 402653696 | bytes 6033573 | solution.py:173
  134.2 1.9 collective-permute-start.1
  137.5 6.2 %body.5 = f32[4,512,128]{2,1,0:T(8,128)S(1)} custom-call(s32[1]{0:T(128)} %bitcast.35.kstart_ref, s32[1,512]{1,0:T(1,128)} %broadcast_in_dim.123.kbias_ref, s32[512,1]{1,0:T(8,128)S(1)} %get-tuple-element.374.seg_ref, s32[512,1]{1,0:T(8,128)} %iota_add_fusion.6.tpos_ref, ...), custom_call_target="tpu_custom_call", output_to_operand_aliasing={{}: (6, {})} | custom-call | flops 402653184 | bytes 2883584 | tf_op jit(solution)/shard_map/while/body/pallas_call | solution.py:60
  143.7 3.4 collective-permute-done.1
  147.8 1.9 collective-permute-start.1
  151.1 6.2 %body.5 = f32[4,512,128]{2,1,0:T(8,128)S(1)} custom-call(s32[1]{0:T(128)} %bitcast.35.kstart_ref, s32[1,512]{1,0:T(1,128)} %broadcast_in_dim.123.kbias_ref, s32[512,1]{1,0:T(8,128)S(1)} %get-tuple-element.374.seg_ref, s32[512,1]{1,0:T(8,128)} %iota_add_fusion.6.tpos_ref, ...), custom_call_target="tpu_custom_call", output_to_operand_aliasing={{}: (6, {})} | custom-call | flops 402653184 | bytes 2883584 | tf_op jit(solution)/shard_map/while/body/pallas_call | solution.py:60
  157.3 3.3 collective-permute-done.1
  161.4 1.9 collective-permute-start.1
  164.7 6.2 %body.5 = f32[4,512,128]{2,1,0:T(8,128)S(1)} custom-call(s32[1]{0:T(128)} %bitcast.35.kstart_ref, s32[1,512]{1,0:T(1,128)} %broadcast_in_dim.123.kbias_ref, s32[512,1]{1,0:T(8,128)S(1)} %get-tuple-element.374.seg_ref, s32[512,1]{1,0:T(8,128)} %iota_add_fusion.6.tpos_ref, ...), custom_call_target="tpu_custom_call", output_to_operand_aliasing={{}: (6, {})} | custom-call | flops 402653184 | bytes 2883584 | tf_op jit(solution)/shard_map/while/body/pallas_call | solution.py:60
  170.9 3.3 collective-permute-done.1
  175.0 1.9 collective-permute-start.1
  178.3 6.2 %body.5 = f32[4,512,128]{2,1,0:T(8,128)S(1)} custom-call(s32[1]{0:T(128)} %bitcast.35.kstart_ref, s32[1,512]{1,0:T(1,128)} %broadcast_in_dim.123.kbias_ref, s32[512,1]{1,0:T(8,128)S(1)} %get-tuple-element.374.seg_ref, s32[512,1]{1,0:T(8,128)} %iota_add_fusion.6.tpos_ref, ...), custom_call_target="tpu_custom_call", output_to_operand_aliasing={{}: (6, {})} | custom-call | flops 402653184 | bytes 2883584 | tf_op jit(solution)/shard_map/while/body/pallas_call | solution.py:60
  184.5 3.3 collective-permute-done.1
  188.6 1.9 collective-permute-start.1
  191.9 6.2 %body.5 = f32[4,512,128]{2,1,0:T(8,128)S(1)} custom-call(s32[1]{0:T(128)} %bitcast.35.kstart_ref, s32[1,512]{1,0:T(1,128)} %broadcast_in_dim.123.kbias_ref, s32[512,1]{1,0:T(8,128)S(1)} %get-tuple-element.374.seg_ref, s32[512,1]{1,0:T(8,128)} %iota_add_fusion.6.tpos_ref, ...), custom_call_target="tpu_custom_call", output_to_operand_aliasing={{}: (6, {})} | custom-call | flops 402653184 | bytes 2883584 | tf_op jit(solution)/shard_map/while/body/pallas_call | solution.py:60
  198.1 3.3 collective-permute-done.1
  202.2 1.9 collective-permute-start.1
  205.5 6.2 %body.5 = f32[4,512,128]{2,1,0:T(8,128)S(1)} custom-call(s32[1]{0:T(128)} %bitcast.35.kstart_ref, s32[1,512]{1,0:T(1,128)} %broadcast_in_dim.123.kbias_ref, s32[512,1]{1,0:T(8,128)S(1)} %get-tuple-element.374.seg_ref, s32[512,1]{1,0:T(8,128)} %iota_add_fusion.6.tpos_ref, ...), custom_call_target="tpu_custom_call", output_to_operand_aliasing={{}: (6, {})} | custom-call | flops 402653184 | bytes 2883584 | tf_op jit(solution)/shard_map/while/body/pallas_call | solution.py:60
  211.7 3.3 collective-permute-done.1
  215.9 1.9 collective-permute-start.1
  219.1 6.2 %body.5 = f32[4,512,128]{2,1,0:T(8,128)S(1)} custom-call(s32[1]{0:T(128)} %bitcast.35.kstart_ref, s32[1,512]{1,0:T(1,128)} %broadcast_in_dim.123.kbias_ref, s32[512,1]{1,0:T(8,128)S(1)} %get-tuple-element.374.seg_ref, s32[512,1]{1,0:T(8,128)} %iota_add_fusion.6.tpos_ref, ...), custom_call_target="tpu_custom_call", output_to_operand_aliasing={{}: (6, {})} | custom-call | flops 402653184 | bytes 2883584 | tf_op jit(solution)/shard_map/while/body/pallas_call | solution.py:60
  225.3 3.4 collective-permute-done.1
  229.5 1.9 collective-permute-start.1
  232.7 6.2 %body.5 = f32[4,512,128]{2,1,0:T(8,128)S(1)} custom-call(s32[1]{0:T(128)} %bitcast.35.kstart_ref, s32[1,512]{1,0:T(1,128)} %broadcast_in_dim.123.kbias_ref, s32[512,1]{1,0:T(8,128)S(1)} %get-tuple-element.374.seg_ref, s32[512,1]{1,0:T(8,128)} %iota_add_fusion.6.tpos_ref, ...), custom_call_target="tpu_custom_call", output_to_operand_aliasing={{}: (6, {})} | custom-call | flops 402653184 | bytes 2883584 | tf_op jit(solution)/shard_map/while/body/pallas_call | solution.py:60
  238.9 3.3 collective-permute-done.1
  243.1 1.9 collective-permute-start.1
  246.3 6.2 %body.5 = f32[4,512,128]{2,1,0:T(8,128)S(1)} custom-call(s32[1]{0:T(128)} %bitcast.35.kstart_ref, s32[1,512]{1,0:T(1,128)} %broadcast_in_dim.123.kbias_ref, s32[512,1]{1,0:T(8,128)S(1)} %get-tuple-element.374.seg_ref, s32[512,1]{1,0:T(8,128)} %iota_add_fusion.6.tpos_ref, ...), custom_call_target="tpu_custom_call", output_to_operand_aliasing={{}: (6, {})} | custom-call | flops 402653184 | bytes 2883584 | tf_op jit(solution)/shard_map/while/body/pallas_call | solution.py:60
  252.5 3.3 collective-permute-done.1
  256.7 1.9 collective-permute-start.1
  259.9 6.2 %body.5 = f32[4,512,128]{2,1,0:T(8,128)S(1)} custom-call(s32[1]{0:T(128)} %bitcast.35.kstart_ref, s32[1,512]{1,0:T(1,128)} %broadcast_in_dim.123.kbias_ref, s32[512,1]{1,0:T(8,128)S(1)} %get-tuple-element.374.seg_ref, s32[512,1]{1,0:T(8,128)} %iota_add_fusion.6.tpos_ref, ...), custom_call_target="tpu_custom_call", output_to_operand_aliasing={{}: (6, {})} | custom-call | flops 402653184 | bytes 2883584 | tf_op jit(solution)/shard_map/while/body/pallas_call | solution.py:60
  266.1 3.3 collective-permute-done.1
  270.3 1.9 collective-permute-start.1
  273.5 6.2 %body.5 = f32[4,512,128]{2,1,0:T(8,128)S(1)} custom-call(s32[1]{0:T(128)} %bitcast.35.kstart_ref, s32[1,512]{1,0:T(1,128)} %broadcast_in_dim.123.kbias_ref, s32[512,1]{1,0:T(8,128)S(1)} %get-tuple-element.374.seg_ref, s32[512,1]{1,0:T(8,128)} %iota_add_fusion.6.tpos_ref, ...), custom_call_target="tpu_custom_call", output_to_operand_aliasing={{}: (6, {})} | custom-call | flops 402653184 | bytes 2883584 | tf_op jit(solution)/shard_map/while/body/pallas_call | solution.py:60
  279.7 3.3 collective-permute-done.1
  283.9 1.9 collective-permute-start.1
  287.1 6.2 %body.5 = f32[4,512,128]{2,1,0:T(8,128)S(1)} custom-call(s32[1]{0:T(128)} %bitcast.35.kstart_ref, s32[1,512]{1,0:T(1,128)} %broadcast_in_dim.123.kbias_ref, s32[512,1]{1,0:T(8,128)S(1)} %get-tuple-element.374.seg_ref, s32[512,1]{1,0:T(8,128)} %iota_add_fusion.6.tpos_ref, ...), custom_call_target="tpu_custom_call", output_to_operand_aliasing={{}: (6, {})} | custom-call | flops 402653184 | bytes 2883584 | tf_op jit(solution)/shard_map/while/body/pallas_call | solution.py:60
  293.3 3.3 collective-permute-done.1
  297.5 1.9 collective-permute-start.1
  300.7 6.2 %body.5 = f32[4,512,128]{2,1,0:T(8,128)S(1)} custom-call(s32[1]{0:T(128)} %bitcast.35.kstart_ref, s32[1,512]{1,0:T(1,128)} %broadcast_in_dim.123.kbias_ref, s32[512,1]{1,0:T(8,128)S(1)} %get-tuple-element.374.seg_ref, s32[512,1]{1,0:T(8,128)} %iota_add_fusion.6.tpos_ref, ...), custom_call_target="tpu_custom_call", output_to_operand_aliasing={{}: (6, {})} | custom-call | flops 402653184 | bytes 2883584 | tf_op jit(solution)/shard_map/while/body/pallas_call | solution.py:60
  306.9 3.3 collective-permute-done.1
  311.1 1.9 collective-permute-start.1
  314.3 6.2 %body.5 = f32[4,512,128]{2,1,0:T(8,128)S(1)} custom-call(s32[1]{0:T(128)} %bitcast.35.kstart_ref, s32[1,512]{1,0:T(1,128)} %broadcast_in_dim.123.kbias_ref, s32[512,1]{1,0:T(8,128)S(1)} %get-tuple-element.374.seg_ref, s32[512,1]{1,0:T(8,128)} %iota_add_fusion.6.tpos_ref, ...), custom_call_target="tpu_custom_call", output_to_operand_aliasing={{}: (6, {})} | custom-call | flops 402653184 | bytes 2883584 | tf_op jit(solution)/shard_map/while/body/pallas_call | solution.py:60
  320.5 3.3 collective-permute-done.1
  324.7 1.9 collective-permute-start.1
  327.9 6.2 %body.5 = f32[4,512,128]{2,1,0:T(8,128)S(1)} custom-call(s32[1]{0:T(128)} %bitcast.35.kstart_ref, s32[1,512]{1,0:T(1,128)} %broadcast_in_dim.123.kbias_ref, s32[512,1]{1,0:T(8,128)S(1)} %get-tuple-element.374.seg_ref, s32[512,1]{1,0:T(8,128)} %iota_add_fusion.6.tpos_ref, ...), custom_call_target="tpu_custom_call", output_to_operand_aliasing={{}: (6, {})} | custom-call | flops 402653184 | bytes 2883584 | tf_op jit(solution)/shard_map/while/body/pallas_call | solution.py:60
  334.1 3.3 collective-permute-done.1
  338.1 6.1 %shard_map.105 = f32[4,512,128]{2,1,0:T(8,128)S(1)} custom-call(s32[1]{0:T(128)} %bitcast.kstart_ref, s32[1,512]{1,0:T(1,128)} %broadcast_in_dim.90.kbias_ref, s32[512,1]{1,0:T(8,128)S(1)} %get-tuple-element.386, s32[512,1]{1,0:T(8,128)} %iota_add_fusion.2.tpos_ref, bf16[4,512,64]{2,1,0:T(8,128)(2,1)S(1)} %get-tuple-element.382, ...), custom_call_target="tpu_custom_call", output_to_operand_aliasing={{}: (6, {})} | custom-call | flops 402653184 | bytes 2883584 | tf_op jit(solution)/shard_map/pallas_call | solution.py:60
  346.2 2.0 copy.58
  349.1 2.3 copy.60
  358.5 20.1 %all-gather.5.cloned.1.call-done = bf16[512,1024]{0,1:T(8,128)(2,1)} async-done(((bf16[512,256]{0,1:T(8,128)(2,1)}), bf16[512,1024]{0,1:T(8,128)(2,1)}) %all-gather.5.cloned.1.call-update) | async-done | bytes 1048592 | tf_op jit(solution)/shard_map/all_gather | solution.py:195
  378.6 2.9 fusion.7
  (114 shorter events, 57.3 us)
Async XLA Ops:
  7.2 57.6 %copy-start = (bf16[2048,256]{1,0:T(8,128)(2,1)S(1)}, bf16[2048,256]{1,0:T(8,128)(2,1)}, u32[]{:S(2)}) copy-start(bf16[2048,256]{1,0:T(8,128)(2,1)} %param.15) | copy-start | bytes 3145732
  7.2 57.6 %copy-start.10 = (f32[2048]{0:T(1024)S(1)}, f32[2048]{0:T(1024)}, u32[]{:S(2)}) copy-start(f32[2048]{0:T(1024)} %param.14) | copy-start | bytes 24580
  7.2 55.3 %all-gather.3.cloned.1.call-start = ((), (), s32[]{:S(2)}) async-start(), calls=%async_computation.1 | async-start | bytes 2621440 | tf_op jit(solution)/shard_map/all_gather | solution.py:106
  62.5 2.3 copy-start.4
  73.6 5.5 %copy-start.7 = (f32[512,32]{1,0:T(8,128)S(1)}, f32[512,32]{1,0:T(8,128)}, u32[]{:S(2)}) copy-start(f32[512,32]{1,0:T(8,128)} %get-tuple-element.239) | copy-start | bytes 196612
  79.1 3.2 copy-start.3
  82.6 13.4 %copy-start.1 = (bf16[512,4,2,64]{3,0,1,2:T(8,128)(2,1)}, bf16[512,4,2,64]{3,0,1,2:T(8,128)(2,1)S(1)}, u32[]{:S(2)}) copy-start(bf16[512,4,2,64]{3,0,1,2:T(8,128)(2,1)S(1)} %pad_maximum_fusion) | copy-start | bytes 1572868
  82.6 4.5 %copy-start.9 = (s32[4]{0:T(128)S(1)}, s32[4]{0:T(128)}, u32[]{:S(2)}) copy-start(s32[4]{0:T(128)} %param.21) | copy-start | bytes 52
  82.6 8.0 %copy-start.8 = (s32[512]{0:T(512)S(1)}, s32[512]{0:T(512)}, u32[]{:S(2)}) copy-start(s32[512]{0:T(512)} %param.19) | copy-start | bytes 6148
  85.2 10.8 %copy-start.5 = (bf16[4,512,128]{2,1,0:T(8,128)(2,1)}, bf16[4,512,128]{2,1,0:T(8,128)(2,1)S(1)}, u32[]{:S(2)}) copy-start(bf16[4,512,128]{2,1,0:T(8,128)(2,1)S(1)} %select_bitcast_fusion.kv_ref) | copy-start | bytes 1572868
  85.2 47.2 %collective-permute-start.2 = (bf16[4,512,128]{2,1,0:T(8,128)(2,1)S(1)}, bf16[4,512,128]{2,1,0:T(8,128)(2,1)}, u32[]{:S(2)}, u32[]{:S(2)}) collective-permute-start(bf16[4,512,128]{2,1,0:T(8,128)(2,1)S(1)} %select_bitcast_fusion.kv_ref), channel_id=1, source_target_pairs={{0,4},{4,8},{8,12},{12,16},{16,20},{20,24},{24,28},{28,32},{32,36}... | collective-permute-start | bytes 1572872 | tf_op jit(solution)/shard_map/ppermute | solution.py:160
  87.1 261.1 %collective-permute-start.3 = (s32[4]{0:T(128)S(1)}, s32[4]{0:T(128)S(1)}, u32[]{:S(2)}, u32[]{:S(2)}) collective-permute-start(s32[4]{0:T(128)S(1)} %copy-done.9), channel_id=1, source_target_pairs={{0,4},{4,8},{8,12},{12,16},{16,20},{20,24},{24,28},{28,32},{32,36}... | collective-permute-start | bytes 56 | tf_op jit(solution)/shard_map/ppermute | solution.py:76
  96.0 253.1 %all-to-all-start = ((bf16[256,4,512]{0,2,1:T(8,128)(2,1)}), bf16[256,4,512]{0,2,1:T(8,128)(2,1)}, u32[]{:S(2)}, u32[]{:S(2)}) async-start(bf16[256,4,512]{0,2,1:T(8,128)(2,1)} %bitcast.15), calls=%async_computation | async-start | bytes 2097152 | tf_op jit(solution)/shard_map/all_to_all | solution.py:132
  100.3 278.4 %all-gather.5.cloned.1.call-start = ((), (), s32[]{:S(2)}) async-start(), calls=%async_computation.2 | async-start | bytes 1310720 | tf_op jit(solution)/shard_map/all_gather | solution.py:195
  134.2 12.8 %collective-permute-start.1 = (bf16[4,512,128]{2,1,0:T(8,128)(2,1)}, bf16[4,512,128]{2,1,0:T(8,128)(2,1)S(1)}, u32[]{:S(2)}, u32[]{:S(2)}) collective-permute-start(bf16[4,512,128]{2,1,0:T(8,128)(2,1)} %copy.86.kv_ref), channel_id=1, source_target_pairs={{0,4},{4,8},{8,12},{12,16},{16,20},{20,24},{24,28},{28,32},{32,36}... | collective-permute-start | bytes 1572872 | tf_op jit(solution)/shard_map/while/body/ppermute | solution.py:166
  147.8 12.8 %collective-permute-start.1 = (bf16[4,512,128]{2,1,0:T(8,128)(2,1)}, bf16[4,512,128]{2,1,0:T(8,128)(2,1)S(1)}, u32[]{:S(2)}, u32[]{:S(2)}) collective-permute-start(bf16[4,512,128]{2,1,0:T(8,128)(2,1)} %copy.86.kv_ref), channel_id=1, source_target_pairs={{0,4},{4,8},{8,12},{12,16},{16,20},{20,24},{24,28},{28,32},{32,36}... | collective-permute-start | bytes 1572872 | tf_op jit(solution)/shard_map/while/body/ppermute | solution.py:166
  161.4 12.8 %collective-permute-start.1 = (bf16[4,512,128]{2,1,0:T(8,128)(2,1)}, bf16[4,512,128]{2,1,0:T(8,128)(2,1)S(1)}, u32[]{:S(2)}, u32[]{:S(2)}) collective-permute-start(bf16[4,512,128]{2,1,0:T(8,128)(2,1)} %copy.86.kv_ref), channel_id=1, source_target_pairs={{0,4},{4,8},{8,12},{12,16},{16,20},{20,24},{24,28},{28,32},{32,36}... | collective-permute-start | bytes 1572872 | tf_op jit(solution)/shard_map/while/body/ppermute | solution.py:166
  175.0 12.8 %collective-permute-start.1 = (bf16[4,512,128]{2,1,0:T(8,128)(2,1)}, bf16[4,512,128]{2,1,0:T(8,128)(2,1)S(1)}, u32[]{:S(2)}, u32[]{:S(2)}) collective-permute-start(bf16[4,512,128]{2,1,0:T(8,128)(2,1)} %copy.86.kv_ref), channel_id=1, source_target_pairs={{0,4},{4,8},{8,12},{12,16},{16,20},{20,24},{24,28},{28,32},{32,36}... | collective-permute-start | bytes 1572872 | tf_op jit(solution)/shard_map/while/body/ppermute | solution.py:166
  188.6 12.8 %collective-permute-start.1 = (bf16[4,512,128]{2,1,0:T(8,128)(2,1)}, bf16[4,512,128]{2,1,0:T(8,128)(2,1)S(1)}, u32[]{:S(2)}, u32[]{:S(2)}) collective-permute-start(bf16[4,512,128]{2,1,0:T(8,128)(2,1)} %copy.86.kv_ref), channel_id=1, source_target_pairs={{0,4},{4,8},{8,12},{12,16},{16,20},{20,24},{24,28},{28,32},{32,36}... | collective-permute-start | bytes 1572872 | tf_op jit(solution)/shard_map/while/body/ppermute | solution.py:166
  202.2 12.8 %collective-permute-start.1 = (bf16[4,512,128]{2,1,0:T(8,128)(2,1)}, bf16[4,512,128]{2,1,0:T(8,128)(2,1)S(1)}, u32[]{:S(2)}, u32[]{:S(2)}) collective-permute-start(bf16[4,512,128]{2,1,0:T(8,128)(2,1)} %copy.86.kv_ref), channel_id=1, source_target_pairs={{0,4},{4,8},{8,12},{12,16},{16,20},{20,24},{24,28},{28,32},{32,36}... | collective-permute-start | bytes 1572872 | tf_op jit(solution)/shard_map/while/body/ppermute | solution.py:166
  215.9 12.8 %collective-permute-start.1 = (bf16[4,512,128]{2,1,0:T(8,128)(2,1)}, bf16[4,512,128]{2,1,0:T(8,128)(2,1)S(1)}, u32[]{:S(2)}, u32[]{:S(2)}) collective-permute-start(bf16[4,512,128]{2,1,0:T(8,128)(2,1)} %copy.86.kv_ref), channel_id=1, source_target_pairs={{0,4},{4,8},{8,12},{12,16},{16,20},{20,24},{24,28},{28,32},{32,36}... | collective-permute-start | bytes 1572872 | tf_op jit(solution)/shard_map/while/body/ppermute | solution.py:166
  229.5 12.8 %collective-permute-start.1 = (bf16[4,512,128]{2,1,0:T(8,128)(2,1)}, bf16[4,512,128]{2,1,0:T(8,128)(2,1)S(1)}, u32[]{:S(2)}, u32[]{:S(2)}) collective-permute-start(bf16[4,512,128]{2,1,0:T(8,128)(2,1)} %copy.86.kv_ref), channel_id=1, source_target_pairs={{0,4},{4,8},{8,12},{12,16},{16,20},{20,24},{24,28},{28,32},{32,36}... | collective-permute-start | bytes 1572872 | tf_op jit(solution)/shard_map/while/body/ppermute | solution.py:166
  243.1 12.8 %collective-permute-start.1 = (bf16[4,512,128]{2,1,0:T(8,128)(2,1)}, bf16[4,512,128]{2,1,0:T(8,128)(2,1)S(1)}, u32[]{:S(2)}, u32[]{:S(2)}) collective-permute-start(bf16[4,512,128]{2,1,0:T(8,128)(2,1)} %copy.86.kv_ref), channel_id=1, source_target_pairs={{0,4},{4,8},{8,12},{12,16},{16,20},{20,24},{24,28},{28,32},{32,36}... | collective-permute-start | bytes 1572872 | tf_op jit(solution)/shard_map/while/body/ppermute | solution.py:166
  256.7 12.8 %collective-permute-start.1 = (bf16[4,512,128]{2,1,0:T(8,128)(2,1)}, bf16[4,512,128]{2,1,0:T(8,128)(2,1)S(1)}, u32[]{:S(2)}, u32[]{:S(2)}) collective-permute-start(bf16[4,512,128]{2,1,0:T(8,128)(2,1)} %copy.86.kv_ref), channel_id=1, source_target_pairs={{0,4},{4,8},{8,12},{12,16},{16,20},{20,24},{24,28},{28,32},{32,36}... | collective-permute-start | bytes 1572872 | tf_op jit(solution)/shard_map/while/body/ppermute | solution.py:166
  270.3 12.8 %collective-permute-start.1 = (bf16[4,512,128]{2,1,0:T(8,128)(2,1)}, bf16[4,512,128]{2,1,0:T(8,128)(2,1)S(1)}, u32[]{:S(2)}, u32[]{:S(2)}) collective-permute-start(bf16[4,512,128]{2,1,0:T(8,128)(2,1)} %copy.86.kv_ref), channel_id=1, source_target_pairs={{0,4},{4,8},{8,12},{12,16},{16,20},{20,24},{24,28},{28,32},{32,36}... | collective-permute-start | bytes 1572872 | tf_op jit(solution)/shard_map/while/body/ppermute | solution.py:166
  283.9 12.8 %collective-permute-start.1 = (bf16[4,512,128]{2,1,0:T(8,128)(2,1)}, bf16[4,512,128]{2,1,0:T(8,128)(2,1)S(1)}, u32[]{:S(2)}, u32[]{:S(2)}) collective-permute-start(bf16[4,512,128]{2,1,0:T(8,128)(2,1)} %copy.86.kv_ref), channel_id=1, source_target_pairs={{0,4},{4,8},{8,12},{12,16},{16,20},{20,24},{24,28},{28,32},{32,36}... | collective-permute-start | bytes 1572872 | tf_op jit(solution)/shard_map/while/body/ppermute | solution.py:166
  297.5 12.8 %collective-permute-start.1 = (bf16[4,512,128]{2,1,0:T(8,128)(2,1)}, bf16[4,512,128]{2,1,0:T(8,128)(2,1)S(1)}, u32[]{:S(2)}, u32[]{:S(2)}) collective-permute-start(bf16[4,512,128]{2,1,0:T(8,128)(2,1)} %copy.86.kv_ref), channel_id=1, source_target_pairs={{0,4},{4,8},{8,12},{12,16},{16,20},{20,24},{24,28},{28,32},{32,36}... | collective-permute-start | bytes 1572872 | tf_op jit(solution)/shard_map/while/body/ppermute | solution.py:166
  311.1 12.8 %collective-permute-start.1 = (bf16[4,512,128]{2,1,0:T(8,128)(2,1)}, bf16[4,512,128]{2,1,0:T(8,128)(2,1)S(1)}, u32[]{:S(2)}, u32[]{:S(2)}) collective-permute-start(bf16[4,512,128]{2,1,0:T(8,128)(2,1)} %copy.86.kv_ref), channel_id=1, source_target_pairs={{0,4},{4,8},{8,12},{12,16},{16,20},{20,24},{24,28},{28,32},{32,36}... | collective-permute-start | bytes 1572872 | tf_op jit(solution)/shard_map/while/body/ppermute | solution.py:166
  324.7 12.8 %collective-permute-start.1 = (bf16[4,512,128]{2,1,0:T(8,128)(2,1)}, bf16[4,512,128]{2,1,0:T(8,128)(2,1)S(1)}, u32[]{:S(2)}, u32[]{:S(2)}) collective-permute-start(bf16[4,512,128]{2,1,0:T(8,128)(2,1)} %copy.86.kv_ref), channel_id=1, source_target_pairs={{0,4},{4,8},{8,12},{12,16},{16,20},{20,24},{24,28},{28,32},{32,36}... | collective-permute-start | bytes 1572872 | tf_op jit(solution)/shard_map/while/body/ppermute | solution.py:166
  344.8 6.5 %copy-start.2 = (bf16[512,4,2,64]{3,0,1,2:T(8,128)(2,1)S(1)}, bf16[512,4,2,64]{3,0,1,2:T(8,128)(2,1)}, u32[]{:S(2)}) copy-start(bf16[512,4,2,64]{3,0,1,2:T(8,128)(2,1)} %copy-done.1) | copy-start | bytes 1572868
  357.4 21.2 %copy-start.6 = (bf16[4,256,512]{2,1,0:T(8,128)(2,1)S(1)}, bf16[4,256,512]{2,1,0:T(8,128)(2,1)}, u32[]{:S(2)}) copy-start(bf16[4,256,512]{2,1,0:T(8,128)(2,1)} %copy.60) | copy-start | bytes 3145732
Sparse Core Ops, SparseCore 0:
  9.8 52.6 all-gather.2
  348.3 30.2 all-gather.4
where the time goes:
time: 390 us; the launch traced here: 388 us
  waiting for transfers between devices  122 us (31%)
  Pallas kernels  106 us (27%)
  local copies, waits for them, and re-layouts  42.3 us (11%)
  starting transfers between devices  38.3 us (10%)
  other arithmetic  29.3 us (8%)
  blocking collectives  22.7 us (6%)
  between operations  17.6 us (5%)
  matrix products  10.1 us (3%)
    pallas_call x17, Pallas kernels, attend_step(): pl.pallas_call(_step_kernel, grid_spec=grid_spec, out_shape=jax.ShapeDtyp...  106 us
    all_gather x1, waiting for transfers between devices, body(): gathered = lax.all_gather(residual, 'tp', axis=1, tiled=True)  50.8 us
    ppermute x15, waiting for transfers between devices, advance(): sent = lax.ppermute(held, 'seq', pairs)  50.2 us
    ppermute x15, starting transfers between devices, advance(): sent = lax.ppermute(held, 'seq', pairs)  28.6 us
    psum x1, blocking collectives, body(): cross_steps = lax.psum(jnp.where(seq_rank == half, cross_here, 0), 'seq')  22.7 us
    all_gather x1, waiting for transfers between devices, body(): attended_all = lax.all_gather(attended, 'tp', axis=1, tiled=True)  20.1 us
    while x15, local copies, waits for them, and re-layouts  11.9 us
    add x16, other arithmetic, body(): places = first_row + jnp.arange(row_count, dtype=jnp.int32)  11.7 us
  transfers between devices with their start and end apart: 20, of which 17 were waited for; matrix products, arithmetic and copies ran while one was open for 15% of the time, Pallas kernels for 27%

commit v1 on v0

--- a/solution.py
+++ b/solution.py
@@ -13,33 +13,63 @@
 THETA = 130000.0
 EPS = 1e-05
 SCALE = HD ** (-0.5)
-
-
-def _step_kernel(kstart_ref, kbias_ref, seg_ref, tpos_ref, q_ref, kv_ref, s_ref, out_ref):
-    q = q_ref[...]
-    kv = kv_ref[...]
+FAR = 1 << 30
+
+
+def _step_kernel(info_ref, valid_ref, seg_ref, q_ref, kv_ref, s_ref, out_ref):
+    kstart = info_ref[0]
+    qstart = info_ref[1]
+    check_valid = info_ref[2]
+    seg_last = info_ref[3]
     rows, width = out_ref.shape
-    keys = kv.shape[0]
-    scores = lax.dot_general(
-        q, kv[:, :HD], (((1,), (1,)), ((), ())), preferred_element_type=jnp.float32
-    ) * SCALE
-    krow = kstart_ref[0] + lax.broadcasted_iota(jnp.int32, (1, keys), 1) + kbias_ref[...]
-    allowed = (krow >= seg_ref[...]) & (krow <= tpos_ref[...])
-    state = s_ref[...]
-    m_old = state[:, 0:1]
-    l_old = state[:, 1:2]
-    block_max = jnp.max(jnp.where(allowed, scores, -1e30), axis=1, keepdims=True)
-    m_new = jnp.maximum(m_old, block_max)
-    weights = jnp.where(allowed, jnp.exp(scores - m_new), 0.0)
-    shrink = jnp.exp(m_old - m_new)
-    l_new = l_old * shrink + jnp.sum(weights, axis=1, keepdims=True)
-    update = jnp.dot(weights.astype(jnp.bfloat16), kv, preferred_element_type=jnp.float32)
-    lane = lax.broadcasted_iota(jnp.int32, (rows, width), 1)
-    acc = state * shrink + update
-    out_ref[...] = jnp.where(lane >= HD, acc, jnp.where(lane == 0, m_new, jnp.where(lane == 1, l_new, 0.0)))
-
-
-def attend_step(kstart, kbias, seg_col, tpos_col, q_hm, kv_hm, state):
+    keys = kv_ref.shape[0]
+    seg_first = seg_ref[0, 0]
+    none_allowed = kstart + keys - 1 < seg_first
+    all_allowed = (seg_last <= kstart) & (kstart + keys - 1 <= qstart) & (check_valid == 0)
+
+    def update(allowed):
+        q = q_ref[...]
+        kv = kv_ref[...]
+        scores = lax.dot_general(
+            q, kv[:, :HD], (((1,), (1,)), ((), ())), preferred_element_type=jnp.float32
+        ) * SCALE
+        state = s_ref[...]
+        m_old = state[:, 0:1]
+        l_old = state[:, 1:2]
+        if allowed is None:
+            block_max = jnp.max(scores, axis=1, keepdims=True)
+        else:
+            block_max = jnp.max(jnp.where(allowed, scores, -1e30), axis=1, keepdims=True)
+        m_new = jnp.maximum(m_old, block_max)
+        weights = jnp.exp(scores - m_new)
+        if allowed is not None:
+            weights = jnp.where(allowed, weights, 0.0)
+        shrink = jnp.exp(m_old - m_new)
+        l_new = l_old * shrink + jnp.sum(weights, axis=1, keepdims=True)
+        pv = jnp.dot(weights.astype(jnp.bfloat16), kv, preferred_element_type=jnp.float32)
+        lane = lax.broadcasted_iota(jnp.int32, (rows, width), 1)
+        acc = state * shrink + pv
+        out_ref[...] = jnp.where(
+            lane >= HD, acc, jnp.where(lane == 0, m_new, jnp.where(lane == 1, l_new, 0.0))
+        )
+
+    @pl.when(none_allowed)
+    def _():
+        out_ref[...] = s_ref[...]
+
+    @pl.when(all_allowed & jnp.logical_not(none_allowed))
+    def _():
+        update(None)
+
+    @pl.when(jnp.logical_not(all_allowed) & jnp.logical_not(none_allowed))
+    def _():
+        kpos = kstart + lax.broadcasted_iota(jnp.int32, (1, keys), 1)
+        kpos = jnp.where((valid_ref[...] > 0) | (check_valid == 0), kpos, FAR)
+        tpos = qstart + lax.broadcasted_iota(jnp.int32, (rows, 1), 0)
+        update((kpos >= seg_ref[...]) & (kpos <= tpos))
+
+
+def attend_step(info, valid_row, seg_col, q_hm, kv_hm, state):
     heads, rows, _ = q_hm.shape
     keys = kv_hm.shape[1]
     width = kv_hm.shape[2]
@@ -47,27 +77,26 @@
         num_scalar_prefetch=1,
         grid=(heads,),
         in_specs=[
-            pl.BlockSpec((1, keys), lambda h, ks: (0, 0)),
-            pl.BlockSpec((rows, 1), lambda h, ks: (0, 0)),
-            pl.BlockSpec((rows, 1), lambda h, ks: (0, 0)),
-            pl.BlockSpec((None, rows, HD), lambda h, ks: (h, 0, 0)),
-            pl.BlockSpec((None, keys, width), lambda h, ks: (h, 0, 0)),
-            pl.BlockSpec((None, rows, width), lambda h, ks: (h, 0, 0)),
+            pl.BlockSpec((1, keys), lambda h, info: (0, 0)),
+            pl.BlockSpec((rows, 1), lambda h, info: (0, 0)),
+            pl.BlockSpec((None, rows, HD), lambda h, info: (h, 0, 0)),
+            pl.BlockSpec((None, keys, width), lambda h, info: (h, 0, 0)),
+            pl.BlockSpec((None, rows, width), lambda h, info: (h, 0, 0)),
         ],
-        out_specs=pl.BlockSpec((None, rows, width), lambda h, ks: (h, 0, 0)),
+        out_specs=pl.BlockSpec((None, rows, width), lambda h, info: (h, 0, 0)),
     )
     flops = heads * rows * keys * (2 * HD + 2 * width)
     return pl.pallas_call(
         _step_kernel,
         grid_spec=grid_spec,
         out_shape=jax.ShapeDtypeStruct(state.shape, jnp.float32),
-        input_output_aliases={6: 0},
+        input_output_aliases={5: 0},
         cost_estimate=pl.CostEstimate(
             flops=flops,
             transcendentals=heads * rows * keys,
             bytes_accessed=q_hm.size * 2 + kv_hm.size * 2 + state.size * 8,
         ),
-    )(kstart, kbias, seg_col, tpos_col, q_hm, kv_hm, state)
+    )(info, valid_row, seg_col, q_hm, kv_hm, state)
 
 
 def passed_along(x, axis, by):
@@ -103,6 +132,18 @@
 ):
     row_count = residual.shape[0]
     local_heads = query_weight.shape[1] // HD
+    seq_rank = lax.axis_index("seq")
+    seq_count = lax.axis_size("seq")
+    reach_dev = min(SPAN, seq_count // 2)
+    half = seq_count // 2
+    chain = [(i, i + 1) for i in range(seq_count - 1)]
+    inner = [p for p in chain if p != (half - 1, half)]
+    first_block = segment_start[0] // row_count
+    cross_here = jnp.clip(seq_rank - first_block, 0, reach_dev).astype(jnp.int32)
+    cross_steps = lax.psum(jnp.where(seq_rank == half, cross_here, 0), "seq")
+
+    cross_steps = jnp.maximum(cross_steps, 1)
+    residual, cross_steps = lax.optimization_barrier((residual, cross_steps))
     gathered = lax.all_gather(residual, "tp", axis=1, tiled=True)
     widened = gathered.astype(jnp.float32)
     mean_sq = jnp.mean(widened * widened, axis=1, keepdims=True)
@@ -135,43 +176,35 @@
     q_hm = jnp.transpose(queries, (1, 0, 2))
     kv_hm = jnp.transpose(packed.reshape(row_count, local_heads, 2 * HD), (1, 0, 2))
     seg_col = segment_start[:, None]
-    tpos_col = places[:, None]
-    own_bias = jnp.where(token_valid > 0, 0, 1 << 30).astype(jnp.int32)[None, :]
-    remote_bias = jnp.zeros((1, row_count), jnp.int32)
-
-    def absorb(state, incoming, step, bias):
-        kstart = (first_row - step * row_count).astype(jnp.int32).reshape(1)
-        return attend_step(kstart, bias, seg_col, tpos_col, q_hm, incoming, state)
+    valid_row = token_valid[None, :]
+    seg_last = segment_start[row_count - 1]
+
+    def absorb(state, incoming, step):
+        info = jnp.stack(
+            [first_row - step * row_count, first_row, (jnp.asarray(step) == 0).astype(jnp.int32), seg_last]
+        ).astype(jnp.int32)
+        return attend_step(info, valid_row, seg_col, q_hm, incoming, state)
 
     lane = jnp.arange(2 * HD, dtype=jnp.int32)
     initial = jnp.broadcast_to(
         jnp.where(lane == 0, -1e30, 0.0).astype(jnp.float32), (local_heads, row_count, 2 * HD)
     )
-    seq_count = lax.axis_size("seq")
-    reach_dev = min(SPAN, seq_count // 2)
-    half = seq_count // 2
-    chain = [(i, i + 1) for i in range(seq_count - 1)]
-    inner = [p for p in chain if p != (half - 1, half)]
-    first_block = segment_start[0] // row_count
-    cross_here = jnp.clip(seq_rank - first_block, 0, reach_dev).astype(jnp.int32)
-    cross_steps = lax.psum(jnp.where(seq_rank == half, cross_here, 0), "seq")
-    cross_steps = jnp.maximum(cross_steps, 1)
 
     prev_block = lax.ppermute(kv_hm, "seq", chain)
-    carried = absorb(initial, kv_hm, 0, own_bias)
+    carried = absorb(initial, kv_hm, 0)
 
     def step_with(pairs):
         def advance(step_index, carry_in):
             held, state = carry_in
             sent = lax.ppermute(held, "seq", pairs)
-            state = absorb(state, held, step_index, remote_bias)
+            state = absorb(state, held, step_index)
             return (sent, state)
 
         return advance
 
     held, carried = lax.fori_loop(1, cross_steps, step_with(chain), (prev_block, carried))
     held, carried = lax.fori_loop(cross_steps, reach_dev, step_with(inner), (held, carried))
-    carried = absorb(carried, held, reach_dev, remote_bias)
+    carried = absorb(carried, held, reach_dev)
     attended = (
         jnp.transpose(carried[:, :, HD:] / carried[:, :, 1:2], (1, 0, 2))
         .astype(jnp.bfloat16)

time: 390 us -> 393 us (level)
  waiting for transfers between devices: 122 us -> 174 us
  Pallas kernels: 106 us -> 58.2 us
  local copies, waits for them, and re-layouts: 42.3 us -> 34.7 us
  other arithmetic: 29.3 us -> 36.7 us
    pallas_call x17, Pallas kernels: 106 us -> 58.2 us  [attend_step(): pl.pallas_call(_step_kernel, grid_spec=grid_spec, out_shape=jax.ShapeDtyp...]
    ppermute x15, waiting for transfers between devices: 50.2 us -> 95.8 us  [advance(): sent = lax.ppermute(held, 'seq', pairs)]
    another operation x0 -> x17, other arithmetic: none -> 20.9 us  [absorb(): jnp.stack([first_row - step * row_count, first_row, (jnp.asarray(step) ==...]
    another operation x0 -> x15, local copies, waits for them, and re-layouts: none -> 11.9 us
    while x15 -> x0, local copies, waits for them, and re-layouts: 11.9 us -> none
    add x16 -> x0, other arithmetic: 11.7 us -> none  [body(): places = first_row + jnp.arange(row_count, dtype=jnp.int32)]
    broadcast_in_dim x16 -> x0, local copies, waits for them, and re-layouts: 9.24 us -> none  [body(): remote_bias = jnp.zeros((1, row_count), jnp.int32)]
    all_gather x1, waiting for transfers between devices: 50.8 us -> 55.3 us  [body(): gathered = lax.all_gather(residual, 'tp', axis=1, tiled=True)]
  transfers between devices with their start and end apart: 20 -> 20, of which waited for: 17 -> 16; matrix products, arithmetic and copies ran while one was open for 15% -> 19% of each run, Pallas kernels for 27% -> 15%
where the time goes in v1:
time: 393 us; the launch traced here: 391 us
  waiting for transfers between devices  174 us (44%)
  Pallas kernels  58.2 us (15%)
  starting transfers between devices  39 us (10%)
  other arithmetic  36.7 us (9%)
  local copies, waits for them, and re-layouts  34.7 us (9%)
  blocking collectives  23.4 us (6%)
  between operations  17.7 us (5%)
  matrix products  7 us (2%)
    ppermute x15, waiting for transfers between devices, advance(): sent = lax.ppermute(held, 'seq', pairs)  95.8 us
    pallas_call x17, Pallas kernels, attend_step(): pl.pallas_call(_step_kernel, grid_spec=grid_spec, out_shape=jax.ShapeDtyp...  58.2 us
    all_gather x1, waiting for transfers between devices, body(): gathered = lax.all_gather(residual, 'tp', axis=1, tiled=True)  55.3 us
    ppermute x15, starting transfers between devices, advance(): sent = lax.ppermute(held, 'seq', pairs)  30.7 us
    psum x1, blocking collectives, body(): cross_steps = lax.psum(jnp.where(seq_rank == half, cross_here, 0), 'seq')  23.4 us
    all_gather x1, waiting for transfers between devices, body(): attended_all = lax.all_gather(attended, 'tp', axis=1, tiled=True)  23.1 us
    another operation x17, other arithmetic, absorb(): jnp.stack([first_row - step * row_count, first_row, (jnp.asarray(step) ==...  20.9 us
    another operation x15, local copies, waits for them, and re-layouts  11.9 us
  transfers between devices with their start and end apart: 20, of which 16 were waited for; matrix products, arithmetic and copies ran while one was open for 19% of the time, Pallas kernels for 15%

profile of v1, /device:TPU:24, one launch (start us, length us, event | category | flops | bytes accessed | tf_op | source)
XLA Modules:
  0.0 391.5 jit_solution(16063523225600084813)
XLA Ops:
  11.3 23.4 %psum.7 = s32[]{:T(128)} all-reduce(s32[]{:T(128)S(6)} %select_n.41), channel_id=1, replica_groups=mesh['seq'=64,'tp'=4] {'seq'}, use_global_device_ids=true, to_apply=%region_0.1 | all-reduce | flops 1 | bytes 8 | tf_op jit(solution)/shard_map/psum | solution.py:143
  35.4 1.9 collective-permute-start.3
  37.3 2.3 copy.59
  39.6 4.4 %all-to-all-start = ((bf16[256,4,512]{0,2,1:T(8,128)(2,1)}), bf16[256,4,512]{0,2,1:T(8,128)(2,1)}, u32[]{:S(2)}, u32[]{:S(2)}) async-start(bf16[256,4,512]{0,2,1:T(8,128)(2,1)} %bitcast.21), calls=%async_computation | async-start | bytes 2097152 | tf_op jit(solution)/shard_map/all_to_all | solution.py:173
  44.1 1.8 multiply_cosine_fusion
  46.0 55.3 %all-gather.3.cloned.1.call-done = bf16[512,2048]{1,0:T(8,128)(2,1)} async-done(((bf16[512,512]{1,0:T(8,128)(2,1)}), bf16[512,2048]{1,0:T(8,128)(2,1)}) %all-gather.3.cloned.1.call-update) | async-done | bytes 2097168 | tf_op jit(solution)/shard_map/all_gather | solution.py:147
  101.3 2.2 fusion
  105.5 2.2 fusion.10
  111.8 2.3 copy.66
  115.4 3.3 fusion.5
  121.6 1.9 collective-permute-start.2
  126.2 1.5 maximum_bitcast_fusion.q_ref
  127.8 9.3 %shard_map.104 = f32[4,512,128]{2,1,0:T(8,128)S(1)} custom-call(s32[4]{0:T(128)} %add_add_fusion.1.info_ref, s32[1,512]{1,0:T(1,128)S(1)} %bitcast.54, s32[512,1]{1,0:T(8,128)S(1)} %copy.57.seg_ref, bf16[4,512,64]{2,1,0:T(8,128)(2,1)S(1)} %maximum_bitcast_fusion.q_ref, bf16[4,512,128]{2,1,0:T(8,128)(2,1)} %copy-done.5, ...), custom_call_target="tpu_custom_call", output_to_operand_aliasing={{}: (5, {})} | custom-call | flops 402653184 | bytes 2883584 | tf_op jit(solution)/shard_map/pallas_call | solution.py:89
  138.2 41.9 %while.24 = (s32[]{:T(128)}, bf16[4,512,128]{2,1,0:T(8,128)(2,1)S(1)}, f32[4,512,128]{2,1,0:T(8,128)S(1)}, s32[]{:T(128)}, s32[]{:T(128)}, /*index=5*/s32[1]{0:T...) while((s32[]{:T(128)}, ...), condition=%wide.region_3.4_spmd, body=%wide.region_2.3_spmd.sunk | while | flops 402653216 | bytes 6029547 | solution.py:205
  139.0 3.3 collective-permute-start
  143.5 9.3 %body.4 = f32[4,512,128]{2,1,0:T(8,128)S(1)} custom-call(s32[4]{0:T(128)} %pad_add_fusion.4.info_ref, s32[1,512]{1,0:T(1,128)S(1)} %get-tuple-element.338.valid_ref, s32[512,1]{1,0:T(8,128)S(1)} %get-tuple-element.339.seg_ref, bf16[4,512,64]{2,1,0:T(8,128)(2,1)S(1)} %get-tuple-element.340.q_ref, ...), custom_call_target="tpu_custom_call", output_to_operand_aliasing={{}: (5, {})} | custom-call | flops 402653184 | bytes 2883584 | tf_op jit(solution)/shard_map/while/body/pallas_call | solution.py:89
  153.7 1.9 collective-permute-start
  156.9 2.8 body.4
  159.6 6.8 %collective-permute-done = bf16[4,512,128]{2,1,0:T(8,128)(2,1)S(1)} collective-permute-done((bf16[4,512,128]{2,1,0:T(8,128)(2,1)}, bf16[4,512,128]{2,1,0:T(8,128)(2,1)S(1)}, u32[]{:S(2)}, u32[]{:S(2)}) %collective-permute-start) | collective-permute-done | bytes 524320 | tf_op jit(solution)/shard_map/while/body/ppermute | solution.py:199
  167.3 2.7 collective-permute-start
  171.2 2.8 body.4
  174.0 6.1 %collective-permute-done = bf16[4,512,128]{2,1,0:T(8,128)(2,1)S(1)} collective-permute-done((bf16[4,512,128]{2,1,0:T(8,128)(2,1)}, bf16[4,512,128]{2,1,0:T(8,128)(2,1)S(1)}, u32[]{:S(2)}, u32[]{:S(2)}) %collective-permute-start) | collective-permute-done | bytes 524320 | tf_op jit(solution)/shard_map/while/body/ppermute | solution.py:199
  180.1 163.2 %while.25 = (s32[]{:T(128)}, bf16[4,512,128]{2,1,0:T(8,128)(2,1)S(1)}, f32[4,512,128]{2,1,0:T(8,128)S(1)}, s32[]{:T(128)}, s32[1]{0:T(128)}, /*index=5*/s32[1,51...) while((s32[]{:T(128)}, ...), condition=%wide.region_5.6_spmd, body=%wide.region_4.5_spmd.sunk | while | flops 402653216 | bytes 6029539 | solution.py:206
  180.9 1.9 collective-permute-start.1
  184.0 2.8 body.5
  186.8 6.9 %collective-permute-done.1 = bf16[4,512,128]{2,1,0:T(8,128)(2,1)S(1)} collective-permute-done((bf16[4,512,128]{2,1,0:T(8,128)(2,1)}, bf16[4,512,128]{2,1,0:T(8,128)(2,1)S(1)}, u32[]{:S(2)}, u32[]{:S(2)}) %collective-permute-start.1) | collective-permute-done | bytes 524320 | tf_op jit(solution)/shard_map/while/body/ppermute | solution.py:199
  194.5 1.9 collective-permute-start.1
  197.6 2.8 body.5
  200.4 6.9 %collective-permute-done.1 = bf16[4,512,128]{2,1,0:T(8,128)(2,1)S(1)} collective-permute-done((bf16[4,512,128]{2,1,0:T(8,128)(2,1)}, bf16[4,512,128]{2,1,0:T(8,128)(2,1)S(1)}, u32[]{:S(2)}, u32[]{:S(2)}) %collective-permute-start.1) | collective-permute-done | bytes 524320 | tf_op jit(solution)/shard_map/while/body/ppermute | solution.py:199
  208.1 1.9 collective-permute-start.1
  211.2 2.8 body.5
  214.0 6.9 %collective-permute-done.1 = bf16[4,512,128]{2,1,0:T(8,128)(2,1)S(1)} collective-permute-done((bf16[4,512,128]{2,1,0:T(8,128)(2,1)}, bf16[4,512,128]{2,1,0:T(8,128)(2,1)S(1)}, u32[]{:S(2)}, u32[]{:S(2)}) %collective-permute-start.1) | collective-permute-done | bytes 524320 | tf_op jit(solution)/shard_map/while/body/ppermute | solution.py:199
  221.7 1.9 collective-permute-start.1
  224.8 2.8 body.5
  227.6 6.9 %collective-permute-done.1 = bf16[4,512,128]{2,1,0:T(8,128)(2,1)S(1)} collective-permute-done((bf16[4,512,128]{2,1,0:T(8,128)(2,1)}, bf16[4,512,128]{2,1,0:T(8,128)(2,1)S(1)}, u32[]{:S(2)}, u32[]{:S(2)}) %collective-permute-start.1) | collective-permute-done | bytes 524320 | tf_op jit(solution)/shard_map/while/body/ppermute | solution.py:199
  235.3 1.9 collective-permute-start.1
  238.4 2.8 body.5
  241.2 6.9 %collective-permute-done.1 = bf16[4,512,128]{2,1,0:T(8,128)(2,1)S(1)} collective-permute-done((bf16[4,512,128]{2,1,0:T(8,128)(2,1)}, bf16[4,512,128]{2,1,0:T(8,128)(2,1)S(1)}, u32[]{:S(2)}, u32[]{:S(2)}) %collective-permute-start.1) | collective-permute-done | bytes 524320 | tf_op jit(solution)/shard_map/while/body/ppermute | solution.py:199
  248.9 1.9 collective-permute-start.1
  252.0 2.8 body.5
  254.8 6.9 %collective-permute-done.1 = bf16[4,512,128]{2,1,0:T(8,128)(2,1)S(1)} collective-permute-done((bf16[4,512,128]{2,1,0:T(8,128)(2,1)}, bf16[4,512,128]{2,1,0:T(8,128)(2,1)S(1)}, u32[]{:S(2)}, u32[]{:S(2)}) %collective-permute-start.1) | collective-permute-done | bytes 524320 | tf_op jit(solution)/shard_map/while/body/ppermute | solution.py:199
  262.5 1.9 collective-permute-start.1
  265.6 2.8 body.5
  268.4 6.9 %collective-permute-done.1 = bf16[4,512,128]{2,1,0:T(8,128)(2,1)S(1)} collective-permute-done((bf16[4,512,128]{2,1,0:T(8,128)(2,1)}, bf16[4,512,128]{2,1,0:T(8,128)(2,1)S(1)}, u32[]{:S(2)}, u32[]{:S(2)}) %collective-permute-start.1) | collective-permute-done | bytes 524320 | tf_op jit(solution)/shard_map/while/body/ppermute | solution.py:199
  276.1 1.9 collective-permute-start.1
  279.2 2.8 body.5
  282.0 6.9 %collective-permute-done.1 = bf16[4,512,128]{2,1,0:T(8,128)(2,1)S(1)} collective-permute-done((bf16[4,512,128]{2,1,0:T(8,128)(2,1)}, bf16[4,512,128]{2,1,0:T(8,128)(2,1)S(1)}, u32[]{:S(2)}, u32[]{:S(2)}) %collective-permute-start.1) | collective-permute-done | bytes 524320 | tf_op jit(solution)/shard_map/while/body/ppermute | solution.py:199
  289.7 1.9 collective-permute-start.1
  292.8 2.8 body.5
  295.6 6.9 %collective-permute-done.1 = bf16[4,512,128]{2,1,0:T(8,128)(2,1)S(1)} collective-permute-done((bf16[4,512,128]{2,1,0:T(8,128)(2,1)}, bf16[4,512,128]{2,1,0:T(8,128)(2,1)S(1)}, u32[]{:S(2)}, u32[]{:S(2)}) %collective-permute-start.1) | collective-permute-done | bytes 524320 | tf_op jit(solution)/shard_map/while/body/ppermute | solution.py:199
  303.3 1.9 collective-permute-start.1
  306.4 2.8 body.5
  309.2 6.9 %collective-permute-done.1 = bf16[4,512,128]{2,1,0:T(8,128)(2,1)S(1)} collective-permute-done((bf16[4,512,128]{2,1,0:T(8,128)(2,1)}, bf16[4,512,128]{2,1,0:T(8,128)(2,1)S(1)}, u32[]{:S(2)}, u32[]{:S(2)}) %collective-permute-start.1) | collective-permute-done | bytes 524320 | tf_op jit(solution)/shard_map/while/body/ppermute | solution.py:199
  316.9 1.9 collective-permute-start.1
  320.0 2.8 body.5
  322.8 6.9 %collective-permute-done.1 = bf16[4,512,128]{2,1,0:T(8,128)(2,1)S(1)} collective-permute-done((bf16[4,512,128]{2,1,0:T(8,128)(2,1)}, bf16[4,512,128]{2,1,0:T(8,128)(2,1)S(1)}, u32[]{:S(2)}, u32[]{:S(2)}) %collective-permute-start.1) | collective-permute-done | bytes 524320 | tf_op jit(solution)/shard_map/while/body/ppermute | solution.py:199
  330.5 1.9 collective-permute-start.1
  333.6 2.8 body.5
  336.4 6.9 %collective-permute-done.1 = bf16[4,512,128]{2,1,0:T(8,128)(2,1)S(1)} collective-permute-done((bf16[4,512,128]{2,1,0:T(8,128)(2,1)}, bf16[4,512,128]{2,1,0:T(8,128)(2,1)S(1)}, u32[]{:S(2)}, u32[]{:S(2)}) %collective-permute-start.1) | collective-permute-done | bytes 524320 | tf_op jit(solution)/shard_map/while/body/ppermute | solution.py:199
  346.4 1.9 copy.58
  349.2 2.3 copy.60
  354.2 1.4 copy.63
  358.7 23.1 %all-gather.5.cloned.1.call-done = bf16[512,1024]{0,1:T(8,128)(2,1)} async-done(((bf16[512,256]{0,1:T(8,128)(2,1)}), bf16[512,1024]{0,1:T(8,128)(2,1)}) %all-gather.5.cloned.1.call-update) | async-done | bytes 1048592 | tf_op jit(solution)/shard_map/all_gather | solution.py:228
  381.8 2.9 fusion.3
  (102 shorter events, 55.4 us)
Async XLA Ops:
  7.2 96.3 %copy-start = (bf16[2048,256]{1,0:T(8,128)(2,1)S(1)}, bf16[2048,256]{1,0:T(8,128)(2,1)}, u32[]{:S(2)}) copy-start(bf16[2048,256]{1,0:T(8,128)(2,1)} %param.17) | copy-start | bytes 3145732
  7.2 94.1 %all-gather.3.cloned.1.call-start = ((), (), s32[]{:S(2)}) async-start(), calls=%async_computation.1 | async-start | bytes 2621440 | tf_op jit(solution)/shard_map/all_gather | solution.py:147
  35.4 8.7 %copy-start.7 = (s32[512]{0:T(512)S(1)}, s32[512]{0:T(512)}, u32[]{:S(2)}) copy-start(s32[512]{0:T(512)} %param.20) | copy-start | bytes 6148
  35.4 8.7 %copy-start.8 = (s32[512]{0:T(512)S(1)}, s32[512]{0:T(512)}, u32[]{:S(2)}) copy-start(s32[512]{0:T(512)} %param.19) | copy-start | bytes 6148
  35.4 312.9 %collective-permute-start.3 = (s32[4]{0:T(128)}, s32[4]{0:T(128)S(1)}, u32[]{:S(2)}, u32[]{:S(2)}) collective-permute-start(s32[4]{0:T(128)} %param.21), channel_id=1, source_target_pairs={{0,4},{4,8},{8,12},{12,16},{16,20},{20,24},{24,28},{28,32},{32,36}... | collective-permute-start | bytes 56 | tf_op jit(solution)/shard_map/ppermute | solution.py:105
  39.6 63.9 %copy-start.11 = (f32[2048]{0:T(1024)S(1)}, f32[2048]{0:T(1024)}, u32[]{:S(2)}) copy-start(f32[2048]{0:T(1024)} %param.14) | copy-start | bytes 24580
  39.6 309.6 %all-to-all-start = ((bf16[256,4,512]{0,2,1:T(8,128)(2,1)}), bf16[256,4,512]{0,2,1:T(8,128)(2,1)}, u32[]{:S(2)}, u32[]{:S(2)}) async-start(bf16[256,4,512]{0,2,1:T(8,128)(2,1)} %bitcast.21), calls=%async_computation | async-start | bytes 2097152 | tf_op jit(solution)/shard_map/all_to_all | solution.py:173
  44.0 337.8 %all-gather.5.cloned.1.call-start = ((), (), s32[]{:S(2)}) async-start(), calls=%async_computation.2 | async-start | bytes 1310720 | tf_op jit(solution)/shard_map/all_gather | solution.py:228
  101.3 2.3 copy-start.4
  105.5 3.0 copy-start.10
  115.4 3.3 copy-start.3
  119.1 8.6 %copy-start.1 = (bf16[512,4,2,64]{3,0,1,2:T(8,128)(2,1)}, bf16[512,4,2,64]{3,0,1,2:T(8,128)(2,1)S(1)}, u32[]{:S(2)}) copy-start(bf16[512,4,2,64]{3,0,1,2:T(8,128)(2,1)S(1)} %pad_maximum_fusion) | copy-start | bytes 1572868
  121.6 6.2 %copy-start.5 = (bf16[4,512,128]{2,1,0:T(8,128)(2,1)}, bf16[4,512,128]{2,1,0:T(8,128)(2,1)S(1)}, u32[]{:S(2)}) copy-start(bf16[4,512,128]{2,1,0:T(8,128)(2,1)S(1)} %select_bitcast_fusion.kv_ref) | copy-start | bytes 1572868
  121.6 15.5 %collective-permute-start.2 = (bf16[4,512,128]{2,1,0:T(8,128)(2,1)S(1)}, bf16[4,512,128]{2,1,0:T(8,128)(2,1)}, u32[]{:S(2)}, u32[]{:S(2)}) collective-permute-start(bf16[4,512,128]{2,1,0:T(8,128)(2,1)S(1)} %select_bitcast_fusion.kv_ref), channel_id=1, source_target_pairs={{0,4},{4,8},{8,12},{12,16},{16,20},{20,24},{24,28},{28,32},{32,36}... | collective-permute-start | bytes 1572872 | tf_op jit(solution)/shard_map/ppermute | solution.py:193
  139.0 13.9 %collective-permute-start = (bf16[4,512,128]{2,1,0:T(8,128)(2,1)}, bf16[4,512,128]{2,1,0:T(8,128)(2,1)S(1)}, u32[]{:S(2)}, u32[]{:S(2)}) collective-permute-start(bf16[4,512,128]{2,1,0:T(8,128)(2,1)} %copy.77.kv_ref), channel_id=1, source_target_pairs={{0,4},{4,8},{8,12},{12,16},{16,20},{20,24},{24,28},{28,32},{32,36}... | collective-permute-start | bytes 1572872 | tf_op jit(solution)/shard_map/while/body/ppermute | solution.py:199
  153.7 12.8 %collective-permute-start = (bf16[4,512,128]{2,1,0:T(8,128)(2,1)}, bf16[4,512,128]{2,1,0:T(8,128)(2,1)S(1)}, u32[]{:S(2)}, u32[]{:S(2)}) collective-permute-start(bf16[4,512,128]{2,1,0:T(8,128)(2,1)} %copy.77.kv_ref), channel_id=1, source_target_pairs={{0,4},{4,8},{8,12},{12,16},{16,20},{20,24},{24,28},{28,32},{32,36}... | collective-permute-start | bytes 1572872 | tf_op jit(solution)/shard_map/while/body/ppermute | solution.py:199
  167.3 12.8 %collective-permute-start = (bf16[4,512,128]{2,1,0:T(8,128)(2,1)}, bf16[4,512,128]{2,1,0:T(8,128)(2,1)S(1)}, u32[]{:S(2)}, u32[]{:S(2)}) collective-permute-start(bf16[4,512,128]{2,1,0:T(8,128)(2,1)} %copy.77.kv_ref), channel_id=1, source_target_pairs={{0,4},{4,8},{8,12},{12,16},{16,20},{20,24},{24,28},{28,32},{32,36}... | collective-permute-start | bytes 1572872 | tf_op jit(solution)/shard_map/while/body/ppermute | solution.py:199
  180.9 12.8 %collective-permute-start.1 = (bf16[4,512,128]{2,1,0:T(8,128)(2,1)}, bf16[4,512,128]{2,1,0:T(8,128)(2,1)S(1)}, u32[]{:S(2)}, u32[]{:S(2)}) collective-permute-start(bf16[4,512,128]{2,1,0:T(8,128)(2,1)} %copy.86.kv_ref), channel_id=1, source_target_pairs={{0,4},{4,8},{8,12},{12,16},{16,20},{20,24},{24,28},{28,32},{32,36}... | collective-permute-start | bytes 1572872 | tf_op jit(solution)/shard_map/while/body/ppermute | solution.py:199
  194.5 12.8 %collective-permute-start.1 = (bf16[4,512,128]{2,1,0:T(8,128)(2,1)}, bf16[4,512,128]{2,1,0:T(8,128)(2,1)S(1)}, u32[]{:S(2)}, u32[]{:S(2)}) collective-permute-start(bf16[4,512,128]{2,1,0:T(8,128)(2,1)} %copy.86.kv_ref), channel_id=1, source_target_pairs={{0,4},{4,8},{8,12},{12,16},{16,20},{20,24},{24,28},{28,32},{32,36}... | collective-permute-start | bytes 1572872 | tf_op jit(solution)/shard_map/while/body/ppermute | solution.py:199
  208.1 12.8 %collective-permute-start.1 = (bf16[4,512,128]{2,1,0:T(8,128)(2,1)}, bf16[4,512,128]{2,1,0:T(8,128)(2,1)S(1)}, u32[]{:S(2)}, u32[]{:S(2)}) collective-permute-start(bf16[4,512,128]{2,1,0:T(8,128)(2,1)} %copy.86.kv_ref), channel_id=1, source_target_pairs={{0,4},{4,8},{8,12},{12,16},{16,20},{20,24},{24,28},{28,32},{32,36}... | collective-permute-start | bytes 1572872 | tf_op jit(solution)/shard_map/while/body/ppermute | solution.py:199
  221.7 12.8 %collective-permute-start.1 = (bf16[4,512,128]{2,1,0:T(8,128)(2,1)}, bf16[4,512,128]{2,1,0:T(8,128)(2,1)S(1)}, u32[]{:S(2)}, u32[]{:S(2)}) collective-permute-start(bf16[4,512,128]{2,1,0:T(8,128)(2,1)} %copy.86.kv_ref), channel_id=1, source_target_pairs={{0,4},{4,8},{8,12},{12,16},{16,20},{20,24},{24,28},{28,32},{32,36}... | collective-permute-start | bytes 1572872 | tf_op jit(solution)/shard_map/while/body/ppermute | solution.py:199
  235.3 12.8 %collective-permute-start.1 = (bf16[4,512,128]{2,1,0:T(8,128)(2,1)}, bf16[4,512,128]{2,1,0:T(8,128)(2,1)S(1)}, u32[]{:S(2)}, u32[]{:S(2)}) collective-permute-start(bf16[4,512,128]{2,1,0:T(8,128)(2,1)} %copy.86.kv_ref), channel_id=1, source_target_pairs={{0,4},{4,8},{8,12},{12,16},{16,20},{20,24},{24,28},{28,32},{32,36}... | collective-permute-start | bytes 1572872 | tf_op jit(solution)/shard_map/while/body/ppermute | solution.py:199
  248.9 12.8 %collective-permute-start.1 = (bf16[4,512,128]{2,1,0:T(8,128)(2,1)}, bf16[4,512,128]{2,1,0:T(8,128)(2,1)S(1)}, u32[]{:S(2)}, u32[]{:S(2)}) collective-permute-start(bf16[4,512,128]{2,1,0:T(8,128)(2,1)} %copy.86.kv_ref), channel_id=1, source_target_pairs={{0,4},{4,8},{8,12},{12,16},{16,20},{20,24},{24,28},{28,32},{32,36}... | collective-permute-start | bytes 1572872 | tf_op jit(solution)/shard_map/while/body/ppermute | solution.py:199
  262.5 12.8 %collective-permute-start.1 = (bf16[4,512,128]{2,1,0:T(8,128)(2,1)}, bf16[4,512,128]{2,1,0:T(8,128)(2,1)S(1)}, u32[]{:S(2)}, u32[]{:S(2)}) collective-permute-start(bf16[4,512,128]{2,1,0:T(8,128)(2,1)} %copy.86.kv_ref), channel_id=1, source_target_pairs={{0,4},{4,8},{8,12},{12,16},{16,20},{20,24},{24,28},{28,32},{32,36}... | collective-permute-start | bytes 1572872 | tf_op jit(solution)/shard_map/while/body/ppermute | solution.py:199
  276.1 12.8 %collective-permute-start.1 = (bf16[4,512,128]{2,1,0:T(8,128)(2,1)}, bf16[4,512,128]{2,1,0:T(8,128)(2,1)S(1)}, u32[]{:S(2)}, u32[]{:S(2)}) collective-permute-start(bf16[4,512,128]{2,1,0:T(8,128)(2,1)} %copy.86.kv_ref), channel_id=1, source_target_pairs={{0,4},{4,8},{8,12},{12,16},{16,20},{20,24},{24,28},{28,32},{32,36}... | collective-permute-start | bytes 1572872 | tf_op jit(solution)/shard_map/while/body/ppermute | solution.py:199
  289.7 12.8 %collective-permute-start.1 = (bf16[4,512,128]{2,1,0:T(8,128)(2,1)}, bf16[4,512,128]{2,1,0:T(8,128)(2,1)S(1)}, u32[]{:S(2)}, u32[]{:S(2)}) collective-permute-start(bf16[4,512,128]{2,1,0:T(8,128)(2,1)} %copy.86.kv_ref), channel_id=1, source_target_pairs={{0,4},{4,8},{8,12},{12,16},{16,20},{20,24},{24,28},{28,32},{32,36}... | collective-permute-start | bytes 1572872 | tf_op jit(solution)/shard_map/while/body/ppermute | solution.py:199
  303.3 12.8 %collective-permute-start.1 = (bf16[4,512,128]{2,1,0:T(8,128)(2,1)}, bf16[4,512,128]{2,1,0:T(8,128)(2,1)S(1)}, u32[]{:S(2)}, u32[]{:S(2)}) collective-permute-start(bf16[4,512,128]{2,1,0:T(8,128)(2,1)} %copy.86.kv_ref), channel_id=1, source_target_pairs={{0,4},{4,8},{8,12},{12,16},{16,20},{20,24},{24,28},{28,32},{32,36}... | collective-permute-start | bytes 1572872 | tf_op jit(solution)/shard_map/while/body/ppermute | solution.py:199
  316.9 12.8 %collective-permute-start.1 = (bf16[4,512,128]{2,1,0:T(8,128)(2,1)}, bf16[4,512,128]{2,1,0:T(8,128)(2,1)S(1)}, u32[]{:S(2)}, u32[]{:S(2)}) collective-permute-start(bf16[4,512,128]{2,1,0:T(8,128)(2,1)} %copy.86.kv_ref), channel_id=1, source_target_pairs={{0,4},{4,8},{8,12},{12,16},{16,20},{20,24},{24,28},{28,32},{32,36}... | collective-permute-start | bytes 1572872 | tf_op jit(solution)/shard_map/while/body/ppermute | solution.py:199
  330.5 12.8 %collective-permute-start.1 = (bf16[4,512,128]{2,1,0:T(8,128)(2,1)}, bf16[4,512,128]{2,1,0:T(8,128)(2,1)S(1)}, u32[]{:S(2)}, u32[]{:S(2)}) collective-permute-start(bf16[4,512,128]{2,1,0:T(8,128)(2,1)} %copy.86.kv_ref), channel_id=1, source_target_pairs={{0,4},{4,8},{8,12},{12,16},{16,20},{20,24},{24,28},{28,32},{32,36}... | collective-permute-start | bytes 1572872 | tf_op jit(solution)/shard_map/while/body/ppermute | solution.py:199
  344.3 4.1 %copy-start.9 = (s32[4]{0:T(128)S(1)}, s32[4]{0:T(128)}, u32[]{:S(2)}) copy-start(s32[4]{0:T(128)} %param.21) | copy-start | bytes 52
  345.0 6.6 %copy-start.2 = (bf16[512,4,2,64]{3,0,1,2:T(8,128)(2,1)S(1)}, bf16[512,4,2,64]{3,0,1,2:T(8,128)(2,1)}, u32[]{:S(2)}) copy-start(bf16[512,4,2,64]{3,0,1,2:T(8,128)(2,1)} %copy-done.1) | copy-start | bytes 1572868
  357.6 24.2 %copy-start.6 = (bf16[4,256,512]{2,1,0:T(8,128)(2,1)S(1)}, bf16[4,256,512]{2,1,0:T(8,128)(2,1)}, u32[]{:S(2)}) copy-start(bf16[4,256,512]{2,1,0:T(8,128)(2,1)} %copy.60) | copy-start | bytes 3145732
Sparse Core Ops, SparseCore 0:
  35.5 65.7 all-gather.2
  348.5 33.2 all-gather.4
